TPU v7x, 128 devices: a whole 4x4x4 slice. The times are simulated.
128 devices in a mesh: dp: 2 (over core), context: 4 (over z), tensor: 16 (over y, x).
Axes of the slice: x: 4, y: 4, z: 4, core: 2. Of those that a mesh axis runs over, the one named last changes fastest.
Arguments:
- tokens: bfloat16 [2, 2048, 8192], P('dp', ('context', 'tensor')), may hold values from -6 to 6
- filter_taps: float32 [2048, 8192], P(('context', 'tensor')), may hold values from -4.5 to 4.5
- query_weight: bfloat16 [32, 256, 256], P('tensor'), may hold values from -0.375 to 0.375
- key_weight: bfloat16 [32, 256, 256], P('tensor'), may hold values from -0.375 to 0.375
- value_weight: bfloat16 [32, 256, 256], P('tensor'), may hold values from -0.375 to 0.375
- output_weight: bfloat16 [32, 256, 256], P('tensor'), may hold values from -0.375 to 0.375
- out_cotangent: bfloat16 [2, 2048, 8192], P('dp', ('context', 'tensor')), may hold values from -6 to 6
Outputs:
- mixed: bfloat16 [2, 2048, 8192], P('dp', ('context', 'tensor'))
- token_grad: bfloat16 [2, 2048, 8192], P('dp', ('context', 'tensor'))
- filter_grad: float32 [2048, 8192], P(('context', 'tensor'))
- query_grad: float32 [32, 256, 256], P('tensor')
- key_grad: float32 [32, 256, 256], P('tensor')
- value_grad: float32 [32, 256, 256], P('tensor')
- output_grad: float32 [32, 256, 256], P('tensor')
All inputs are finite; a program needn't handle non-finite values.
Results may differ from a plain program's by a relative error of at most 0.02.
Values may be sent and summed in bfloat16 or wider, within the bound.
No kernel may reach another device: no remote copies, remote signals or barrier semaphores. Data moves between devices by JAX's collectives and lax.ppermute only.
A program may use at most 128 MiB of HBM per device.

v0:
```python
import math

import jax
import jax.numpy as jnp
from jax import lax
from jax.sharding import PartitionSpec as P

table_mode = lax.Precision.HIGH


def blockwise(acts, weight):
    rows = acts.shape[0]
    shaped = acts.reshape(rows, weight.shape[0], weight.shape[1])
    return jnp.einsum("tni,nij->tnj", shaped, weight, preferred_element_type=jnp.float32).reshape(
        rows, -1
    )


def blockwise_back(acts, weight):
    rows = acts.shape[0]
    shaped = acts.reshape(rows, weight.shape[0], weight.shape[1])
    return jnp.einsum("tnj,nij->tni", shaped, weight, preferred_element_type=jnp.float32).reshape(
        rows, -1
    )


def weight_term(inputs, grads, blocks):
    rows = inputs.shape[0]
    left = inputs.reshape(rows, blocks, -1)
    right = grads.reshape(rows, blocks, -1)
    return jnp.einsum("tni,tnj->nij", left, right, preferred_element_type=jnp.float32)


def angle_table(rows, cols, total):
    product = (
        jnp.arange(rows, dtype=jnp.int32)[:, None]
        * jnp.arange(cols, dtype=jnp.int32)[None, :]
        % total
    )
    angle = product.astype(jnp.float32) * (2.0 * math.pi / total)
    return (jnp.cos(angle), jnp.sin(angle))


def make_tables(length):
    second = length // 128
    cosine_first, sine_first = angle_table(128, 128, 128)
    cosine_second, sine_second = angle_table(second, second, second)
    cosine_twist, sine_twist = angle_table(128, second, length)
    return (
        cosine_first,
        sine_first,
        cosine_second,
        sine_second,
        cosine_twist[:, :, None],
        sine_twist[:, :, None],
    )


def across_first(matrix, array):
    return jnp.einsum(
        "kn,nmc->kmc", matrix, array, precision=table_mode, preferred_element_type=jnp.float32
    )


def across_second(array, matrix):
    return jnp.einsum(
        "kmc,ml->klc", array, matrix, precision=table_mode, preferred_element_type=jnp.float32
    )


def forward_transform(signal, tables):
    cosine_first, sine_first, cosine_second, sine_second, cosine_twist, sine_twist = tables
    half = cosine_first.shape[0] // 2
    shaped = signal.reshape(half, cosine_second.shape[0], signal.shape[1])
    real_section = across_first(cosine_first[:, :half], shaped)
    imag_section = -across_first(sine_first[:, :half], shaped)
    real_turned = real_section * cosine_twist + imag_section * sine_twist
    imag_turned = imag_section * cosine_twist - real_section * sine_twist
    real_out = across_second(real_turned, cosine_second) + across_second(imag_turned, sine_second)
    imag_out = across_second(imag_turned, cosine_second) - across_second(real_turned, sine_second)
    return (real_out, imag_out)


def inverse_transform(real_spec, imag_spec, tables):
    cosine_first, sine_first, cosine_second, sine_second, cosine_twist, sine_twist = tables
    half = cosine_first.shape[0] // 2
    total = cosine_first.shape[0] * cosine_second.shape[0]
    real_section = across_second(real_spec, cosine_second) - across_second(imag_spec, sine_second)
    imag_section = across_second(imag_spec, cosine_second) + across_second(real_spec, sine_second)
    real_turned = real_section * cosine_twist - imag_section * sine_twist
    imag_turned = imag_section * cosine_twist + real_section * sine_twist
    signal = (
        across_first(cosine_first[:half], real_turned)
        - across_first(sine_first[:half], imag_turned)
    ) / total
    return signal.reshape(half * cosine_second.shape[0], -1)


def shards(
    tokens, filter_taps, query_weight, key_weight, value_weight, output_weight, out_cotangent
):
    inputs, upstream = (
        lax.all_to_all(tokens[0], "tensor", split_axis=1, concat_axis=0, tiled=True),
        lax.all_to_all(out_cotangent[0], "tensor", split_axis=1, concat_axis=0, tiled=True),
    )
    blocks = query_weight.shape[0]
    query = blockwise(inputs, query_weight).astype(jnp.bfloat16)
    keys = blockwise(inputs, key_weight).astype(jnp.bfloat16)
    values = blockwise(inputs, value_weight).astype(jnp.bfloat16)
    gated = (keys.astype(jnp.float32) * values.astype(jnp.float32)).astype(jnp.bfloat16)
    query_wide = query.astype(jnp.float32)
    taps = lax.all_to_all(
        lax.all_to_all(filter_taps, "tensor", split_axis=1, concat_axis=0, tiled=True),
        "context",
        split_axis=1,
        concat_axis=0,
        tiled=True,
    )
    length = taps.shape[0]
    tables = make_tables(2 * length)
    gated_time = lax.all_to_all(gated, "context", split_axis=1, concat_axis=0, tiled=True)
    real_taps, imag_taps = forward_transform(taps, tables)
    real_gated, imag_gated = forward_transform(gated_time.astype(jnp.float32), tables)
    conv_time = inverse_transform(
        real_taps * real_gated - imag_taps * imag_gated,
        real_taps * imag_gated + imag_taps * real_gated,
        tables,
    )
    conv = lax.all_to_all(
        conv_time.astype(jnp.bfloat16), "context", split_axis=0, concat_axis=1, tiled=True
    )
    back_weighted = blockwise_back(upstream, output_weight)
    conv_grad = (back_weighted * query_wide).astype(jnp.bfloat16)
    grad_time = lax.all_to_all(conv_grad, "context", split_axis=1, concat_axis=0, tiled=True)
    real_grad, imag_grad = forward_transform(grad_time.astype(jnp.float32), tables)
    gated_time_back = inverse_transform(
        real_taps * real_grad + imag_taps * imag_grad,
        real_taps * imag_grad - imag_taps * real_grad,
        tables,
    )
    taps_back = inverse_transform(
        real_grad * real_gated + imag_grad * imag_gated,
        imag_grad * real_gated - real_grad * imag_gated,
        tables,
    )
    gated_narrow = lax.all_to_all(
        gated_time_back.astype(jnp.bfloat16), "context", split_axis=0, concat_axis=1, tiled=True
    )
    conv_wide = conv.astype(jnp.float32)
    weighted = (query_wide * conv_wide).astype(jnp.bfloat16)
    mixed = blockwise(weighted, output_weight).astype(jnp.bfloat16)
    mixed_rows = lax.all_to_all(mixed, "tensor", split_axis=0, concat_axis=1, tiled=True)
    query_back = (back_weighted * conv_wide).astype(jnp.bfloat16)
    gated_back = gated_narrow.astype(jnp.float32)
    key_back = (gated_back * values.astype(jnp.float32)).astype(jnp.bfloat16)
    value_back = (gated_back * keys.astype(jnp.float32)).astype(jnp.bfloat16)
    token_grad = (
        blockwise_back(query_back, query_weight)
        + blockwise_back(key_back, key_weight)
        + blockwise_back(value_back, value_weight)
    ).astype(jnp.bfloat16)
    factor = 1.0 / math.sqrt(lax.axis_size("dp") * length)
    query_grad, key_grad, value_grad, output_grad = (
        lax.psum(
            (weight_term(inputs, query_back, blocks) * factor).astype(jnp.bfloat16),
            ("dp", "context"),
        ).astype(jnp.float32),
        lax.psum(
            (weight_term(inputs, key_back, blocks) * factor).astype(jnp.bfloat16), ("dp", "context")
        ).astype(jnp.float32),
        lax.psum(
            (weight_term(inputs, value_back, blocks) * factor).astype(jnp.bfloat16),
            ("dp", "context"),
        ).astype(jnp.float32),
        lax.psum(
            (weight_term(weighted, upstream, blocks) * factor).astype(jnp.bfloat16),
            ("dp", "context"),
        ).astype(jnp.float32),
    )
    taps_total = lax.psum((taps_back * factor).astype(jnp.bfloat16), "dp").astype(jnp.float32)
    filter_grad = lax.all_to_all(
        lax.all_to_all(
            taps_total.astype(jnp.bfloat16), "context", split_axis=0, concat_axis=1, tiled=True
        ),
        "tensor",
        split_axis=0,
        concat_axis=1,
        tiled=True,
    ).astype(taps_total.dtype)
    grad_rows = lax.all_to_all(token_grad, "tensor", split_axis=0, concat_axis=1, tiled=True)
    return (
        mixed_rows[None],
        grad_rows[None],
        filter_grad,
        query_grad,
        key_grad,
        value_grad,
        output_grad,
    )


def solution(mesh):
    placed = (
        P("dp", ("context", "tensor"), None),
        P(("context", "tensor"), None),
        P("tensor", None, None),
        P("tensor", None, None),
        P("tensor", None, None),
        P("tensor", None, None),
        P("dp", ("context", "tensor"), None),
    )
    return jax.shard_map(
        shards,
        mesh=mesh,
        in_specs=placed,
        out_specs=(
            P("dp", ("context", "tensor"), None),
            P("dp", ("context", "tensor"), None),
            P(("context", "tensor"), None),
            P("tensor", None, None),
            P("tensor", None, None),
            P("tensor", None, None),
            P("tensor", None, None),
        ),
        check_vma=False,
    )
```

profile of v0, /device:TPU:0, one launch (start us, length us, event | category | flops | bytes accessed | tf_op | source)
XLA Modules:
  0.0 347.2 jit_solution(17695907332183723732)
XLA Ops:
  10.4 7.1 %all-to-all-start = ((bf16[32,16,512]{2,0,1:T(8,128)(2,1)}), bf16[32,16,512]{2,0,1:T(8,128)(2,1)S(1)}, u32[]{:S(2)}, u32[]{:S(2)}) async-start(bf16[32,16,512]{2,0,1:T(8,128)(2,1)} %copy.193), calls=%async_computation | async-start | bytes 1048576 | tf_op jit(solution)/shard_map/all_to_all | solution.py:103
  18.8 10.2 %all-to-all-done = bf16[32,16,512]{2,0,1:T(8,128)(2,1)S(1)} async-done(((bf16[32,16,512]{2,0,1:T(8,128)(2,1)}), bf16[32,16,512]{2,0,1:T(8,128)(2,1)S(1)}, u32[]{:S(2)}, u32[]{:S(2)}) %all-to-all-start) | async-done | bytes 524320 | tf_op jit(solution)/shard_map/all_to_all | solution.py:103
  36.1 7.0 %all-to-all-done.6 = bf16[32,16,512]{2,0,1:T(8,128)(2,1)S(1)} async-done(((bf16[32,16,512]{2,0,1:T(8,128)(2,1)}), bf16[32,16,512]{2,0,1:T(8,128)(2,1)S(1)}, u32[]{:S(2)}, u32[]{:S(2)}) %all-to-all-start.6) | async-done | bytes 524320 | tf_op jit(solution)/shard_map/all_to_all | solution.py:104
  43.1 5.3 %all-to-all-start.3 = ((bf16[512,4,128]{2,0,1:T(8,128)(2,1)}), bf16[512,4,128]{2,0,1:T(8,128)(2,1)S(1)}, u32[]{:S(2)}, u32[]{:S(2)}) async-start(bf16[512,4,128]{2,0,1:T(8,128)(2,1)} %copy.206), calls=%async_computation.3 | async-start | bytes 1048576 | tf_op jit(solution)/shard_map/all_to_all | solution.py:121
  50.8 5.7 %all-to-all-done.3 = bf16[512,4,128]{2,0,1:T(8,128)(2,1)S(1)} async-done(((bf16[512,4,128]{2,0,1:T(8,128)(2,1)}), bf16[512,4,128]{2,0,1:T(8,128)(2,1)S(1)}, u32[]{:S(2)}, u32[]{:S(2)}) %all-to-all-start.3) | async-done | bytes 524320 | tf_op jit(solution)/shard_map/all_to_all | solution.py:121
  56.5 3.7 %all-to-all-start.1 = ((f32[32,16,512]{2,0,1:T(8,128)}), f32[32,16,512]{2,0,1:T(8,128)S(1)}, u32[]{:S(2)}, u32[]{:S(2)}) async-start(f32[32,16,512]{2,0,1:T(8,128)} %bitcast.289), calls=%async_computation.1 | async-start | bytes 2097152 | tf_op jit(solution)/shard_map/all_to_all | solution.py:113
  64.8 9.7 %all-to-all-done.1 = f32[32,16,512]{2,0,1:T(8,128)S(1)} async-done(((f32[32,16,512]{2,0,1:T(8,128)}), f32[32,16,512]{2,0,1:T(8,128)S(1)}, u32[]{:S(2)}, u32[]{:S(2)}) %all-to-all-start.1) | async-done | bytes 1048608 | tf_op jit(solution)/shard_map/all_to_all | solution.py:113
  82.8 4.2 %all-to-all-done.7 = bf16[512,4,128]{2,0,1:T(8,128)(2,1)S(1)} async-done(((bf16[512,4,128]{2,0,1:T(8,128)(2,1)}), bf16[512,4,128]{2,0,1:T(8,128)(2,1)S(1)}, u32[]{:S(2)}, u32[]{:S(2)}) %all-to-all-start.7) | async-done | bytes 524320 | tf_op jit(solution)/shard_map/all_to_all | solution.py:134
  97.0 4.3 %all-to-all-done.2 = f32[512,4,128]{2,0,1:T(8,128)S(1)} async-done(((f32[512,4,128]{2,0,1:T(8,128)}), f32[512,4,128]{2,0,1:T(8,128)S(1)}, u32[]{:S(2)}, u32[]{:S(2)}) %all-to-all-start.2) | async-done | bytes 1048608 | tf_op jit(solution)/shard_map/all_to_all | solution.py:112
  134.5 6.3 %multiply_add_fusion = (f32[32,128,128]{2,0,1:T(8,128)S(1)}, f32[32,128,128]{2,0,1:T(8,128)S(1)}, f32[32,128,128]{2,0,1:T(8,128)S(1)}, f32[32,128,128]{2,0,1:T(8...) fusion(f32[32,128,128]{2,0,1:T(8,128)S(1)} %fusion.75, f32[32,128,128]{2,0,1:T(8,128)} %fusion.78, ...), kind=kOutput, calls=%fused_computation.55 | convolution fusion | flops 110639104 | bytes 27262976 | tf_op jit(solution)/shard_map/kmc,ml->klc/dot_general | solution.py:66
  163.4 6.6 %fusion.1 = f32[64,32,128]{2,0,1:T(8,128)S(1)} fusion(f32[128,32]{0,1:T(8,128)S(1)} %get-tuple-element.67, f32[128,32]{0,1:T(8,128)S(1)} %copy-done.32, f32[32,128,128]{2,0,1:T(8,128)S(1)} %fusion.8, f32[32,128,128]{2,0,1:T(8,128)S(1)} %fusion.12, f32[32,128,128]{2,0,1:T(8,128)S(1)} %fusion.10, f32[32,128,128]{2,0,1:T(8,128)S(1)} %fusion.6, ...), kind=kOutput, calls=%fused_computation.3 | convolution fusion | flops 203948032 | bytes 9535488 | tf_op jit(solution)/shard_map/kn,nmc->kmc/dot_general | solution.py:60
  170.1 9.7 %fusion.108 = bf16[64,32,128]{2,0,1:T(8,128)(2,1)S(1)} fusion(f32[64,32,128]{2,0,1:T(8,128)S(1)} %fusion.1, f32[128,32]{0,1:T(8,128)S(1)} %get-tuple-element.67, f32[128,32]{0,1:T(8,128)S(1)} %copy-done.32, f32[32,128,128]{2,0,1:T(8,128)S(1)} %fusion.8, f32[32,128,128]{2,0,1:T(8,128)S(1)} %fusion.12, f32[32,128,128]{2,0,1:T(8,128)S(1)} %fusion.10, ...), kind=kOutput, calls=%fused_computation.110 | convolution fusion | flops 204734464 | bytes 10059776 | tf_op jit(solution)/shard_map/kn,nmc->kmc/dot_general | solution.py:60
  181.0 7.9 %fusion.29 = f32[64,32,128]{2,0,1:T(8,128)S(1)} fusion(f32[128,32]{0,1:T(8,128)S(1)} %get-tuple-element.67, f32[128,32]{0,1:T(8,128)} %get-tuple-element.68, f32[32,128,128]{2,0,1:T(8,128)} %fusion.36, f32[32,128,128]{2,0,1:T(8,128)} %fusion.40, f32[32,128,128]{2,0,1:T(8,128)} %fusion.38, f32[32,128,128]{2,0,1:T(8,128)} %fusion.34, f32[128,128]{0,1:T(8,128)S(1)} %fusion.169), kind=kOutput, calls=%fused_computation.35 | convolution fusion | flops 203948032 | bytes 9535488 | tf_op jit(solution)/shard_map/kn,nmc->kmc/dot_general | solution.py:60
  188.9 9.7 %fusion.102 = bf16[64,32,128]{2,0,1:T(8,128)(2,1)S(1)} fusion(f32[64,32,128]{2,0,1:T(8,128)S(1)} %fusion.29, f32[128,32]{0,1:T(8,128)S(1)} %get-tuple-element.67, f32[128,32]{0,1:T(8,128)S(1)} %copy-done.33, f32[32,128,128]{2,0,1:T(8,128)S(1)} %copy-done.5, f32[32,128,128]{2,0,1:T(8,128)S(1)} %copy-done.7, f32[32,128,128]{2,0,1:T(8,128)S(1)} %copy-done.6, ...), kind=kOutput, calls=%fused_computation.108 | convolution fusion | flops 204734464 | bytes 10059776 | tf_op jit(solution)/shard_map/kn,nmc->kmc/dot_general | solution.py:60
  199.7 4.1 %all-to-all-start.4 = ((bf16[4,512,128]{2,1,0:T(8,128)(2,1)}), bf16[4,512,128]{2,1,0:T(8,128)(2,1)}, u32[]{:S(2)}, u32[]{:S(2)}) async-start(bf16[4,512,128]{2,1,0:T(8,128)(2,1)} %bitcast.306), calls=%async_computation.4 | async-start | bytes 1048576 | tf_op jit(solution)/shard_map/all_to_all | solution.py:129
  203.9 7.3 %fusion.15 = f32[64,32,128]{2,0,1:T(8,128)S(1)} fusion(f32[128,32]{0,1:T(8,128)S(1)} %get-tuple-element.67, f32[128,32]{0,1:T(8,128)} %get-tuple-element.68, f32[32,128,128]{2,0,1:T(8,128)} %fusion.22, f32[32,128,128]{2,0,1:T(8,128)} %fusion.26, f32[32,128,128]{2,0,1:T(8,128)} %fusion.24, f32[32,128,128]{2,0,1:T(8,128)S(1)} %fusion.20, ...), kind=kOutput, calls=%fused_computation.19 | convolution fusion | flops 203948032 | bytes 9535488 | tf_op jit(solution)/shard_map/kn,nmc->kmc/dot_general | solution.py:60
  211.3 9.7 %fusion.105 = bf16[64,32,128]{2,0,1:T(8,128)(2,1)S(1)} fusion(f32[64,32,128]{2,0,1:T(8,128)S(1)} %fusion.15, f32[128,32]{0,1:T(8,128)S(1)} %get-tuple-element.67, f32[128,32]{0,1:T(8,128)S(1)} %copy-done.34, f32[32,128,128]{2,0,1:T(8,128)S(1)} %copy-done.1, f32[32,128,128]{2,0,1:T(8,128)S(1)} %copy-done.3, f32[32,128,128]{2,0,1:T(8,128)S(1)} %copy-done.2, ...), kind=kOutput, calls=%fused_computation.109 | convolution fusion | flops 204734464 | bytes 10059776 | tf_op jit(solution)/shard_map/kn,nmc->kmc/dot_general | solution.py:60
  222.1 4.9 %all-to-all-start.8 = ((bf16[4,512,128]{2,1,0:T(8,128)(2,1)}), bf16[4,512,128]{2,1,0:T(8,128)(2,1)}, u32[]{:S(2)}, u32[]{:S(2)}) async-start(bf16[4,512,128]{2,1,0:T(8,128)(2,1)} %bitcast.38), calls=%async_computation.8 | async-start | bytes 1048576 | tf_op jit(solution)/shard_map/all_to_all | solution.py:146
  235.4 3.6 %all-to-all-start.5 = ((bf16[16,32,512]{2,1,0:T(8,128)(2,1)}), bf16[16,32,512]{2,1,0:T(8,128)(2,1)S(1)}, u32[]{:S(2)}, u32[]{:S(2)}) async-start(bf16[16,32,512]{2,1,0:T(8,128)(2,1)} %convert_element_type.345), calls=%async_computation.5 | async-start | bytes 1048576 | tf_op jit(solution)/shard_map/all_to_all | solution.py:152
  245.2 3.9 %all-to-all-done.5 = bf16[16,32,512]{2,1,0:T(8,128)(2,1)S(1)} async-done(((bf16[16,32,512]{2,1,0:T(8,128)(2,1)}), bf16[16,32,512]{2,1,0:T(8,128)(2,1)S(1)}, u32[]{:S(2)}, u32[]{:S(2)}) %all-to-all-start.5) | async-done | bytes 524320 | tf_op jit(solution)/shard_map/all_to_all | solution.py:152
  249.1 4.8 %all-to-all-start.10 = ((bf16[4,512,128]{2,1,0:T(8,128)(2,1)}), bf16[4,512,128]{2,1,0:T(8,128)(2,1)S(1)}, u32[]{:S(2)}, u32[]{:S(2)}) async-start(bf16[4,512,128]{2,1,0:T(8,128)(2,1)} %all-reduce.4.cloned.1.call-done), calls=%async_computation.10 | async-start | bytes 1048576 | tf_op jit(solution)/shard_map/all_to_all | solution.py:182
  257.0 5.0 %all-to-all-done.10 = bf16[4,512,128]{2,1,0:T(8,128)(2,1)S(1)} async-done(((bf16[4,512,128]{2,1,0:T(8,128)(2,1)}), bf16[4,512,128]{2,1,0:T(8,128)(2,1)S(1)}, u32[]{:S(2)}, u32[]{:S(2)}) %all-to-all-start.10) | async-done | bytes 524320 | tf_op jit(solution)/shard_map/all_to_all | solution.py:182
  270.1 6.7 %all-to-all-done.9 = bf16[16,32,512]{2,1,0:T(8,128)(2,1)S(1)} async-done(((bf16[16,32,512]{2,1,0:T(8,128)(2,1)}), bf16[16,32,512]{2,1,0:T(8,128)(2,1)S(1)}, u32[]{:S(2)}, u32[]{:S(2)}) %all-to-all-start.9) | async-done | bytes 524320 | tf_op jit(solution)/shard_map/all_to_all | solution.py:190
  283.1 48.8 %all-reduce.6.cloned.1.call-done = (bf16[2,256,256]{1,2,0:T(8,128)(2,1)}, bf16[2,256,256]{1,2,0:T(8,128)(2,1)}, bf16[2,256,256]{1,2,0:T(8,128)(2,1)}, bf16[2,256,256]{2,1,0:T(8,128)(2,1)}) async-done(((bf16[2,256,256]{1,2,0:T(8,128)(2,1)}, bf16[2,256,256]{1,2,0:T(8,128)(2,1)}, bf16[2,256,256]{1,2,0:T(8,128)(2,1)}, bf16[2,256,256]{2,1,0:T(8,128)(2,1)}), (bf16[2,256,256]{1,2,0:T(8,128)(2,1)}, ...) | async-done | bytes 1048592 | tf_op jit(solution)/shard_map/psum | solution.py:164
  (167 shorter events, 134.6 us)
Async XLA Ops:
  8.0 54.4 %copy-start = (bf16[2,256,256]{2,1,0:T(8,128)(2,1)S(1)}, bf16[2,256,256]{2,1,0:T(8,128)(2,1)}, u32[]{:S(2)}) copy-start(bf16[2,256,256]{2,1,0:T(8,128)(2,1)} %param.12) | copy-start | bytes 786436
  8.0 9.5 %copy-start.35 = (bf16[1,32,8192]{2,1,0:T(8,128)(2,1)S(1)}, bf16[1,32,8192]{2,1,0:T(8,128)(2,1)}, u32[]{:S(2)}) copy-start(bf16[1,32,8192]{2,1,0:T(8,128)(2,1)} %param.13) | copy-start | bytes 1572868
  10.4 18.7 %all-to-all-start = ((bf16[32,16,512]{2,0,1:T(8,128)(2,1)}), bf16[32,16,512]{2,0,1:T(8,128)(2,1)S(1)}, u32[]{:S(2)}, u32[]{:S(2)}) async-start(bf16[32,16,512]{2,0,1:T(8,128)(2,1)} %copy.193), calls=%async_computation | async-start | bytes 1048576 | tf_op jit(solution)/shard_map/all_to_all | solution.py:103
  17.6 15.2 %copy-start.29 = (bf16[2,256,256]{2,1,0:T(8,128)(2,1)S(1)}, bf16[2,256,256]{2,1,0:T(8,128)(2,1)}, u32[]{:S(2)}) copy-start(bf16[2,256,256]{2,1,0:T(8,128)(2,1)} %param.10) | copy-start | bytes 786436
  17.7 16.2 %copy-start.27 = (bf16[2,256,256]{2,1,0:T(8,128)(2,1)S(1)}, bf16[2,256,256]{2,1,0:T(8,128)(2,1)}, u32[]{:S(2)}) copy-start(bf16[2,256,256]{2,1,0:T(8,128)(2,1)} %param.11) | copy-start | bytes 786436
  29.1 14.0 %all-to-all-start.6 = ((bf16[32,16,512]{2,0,1:T(8,128)(2,1)}), bf16[32,16,512]{2,0,1:T(8,128)(2,1)S(1)}, u32[]{:S(2)}, u32[]{:S(2)}) async-start(bf16[32,16,512]{2,0,1:T(8,128)(2,1)} %copy.226), calls=%async_computation.6 | async-start | bytes 1048576 | tf_op jit(solution)/shard_map/all_to_all | solution.py:104
  32.8 28.3 %copy-start.11 = (bf16[512,2,256]{2,1,0:T(2,128)(2,1)}, bf16[512,2,256]{2,1,0:T(2,128)(2,1)S(1)}, u32[]{:S(2)}) copy-start(bf16[512,2,256]{2,1,0:T(2,128)(2,1)S(1)} %reshape.176) | copy-start | bytes 1572868
  43.1 13.4 %all-to-all-start.3 = ((bf16[512,4,128]{2,0,1:T(8,128)(2,1)}), bf16[512,4,128]{2,0,1:T(8,128)(2,1)S(1)}, u32[]{:S(2)}, u32[]{:S(2)}) async-start(bf16[512,4,128]{2,0,1:T(8,128)(2,1)} %copy.206), calls=%async_computation.3 | async-start | bytes 1048576 | tf_op jit(solution)/shard_map/all_to_all | solution.py:121
  56.5 17.9 %all-to-all-start.1 = ((f32[32,16,512]{2,0,1:T(8,128)}), f32[32,16,512]{2,0,1:T(8,128)S(1)}, u32[]{:S(2)}, u32[]{:S(2)}) async-start(f32[32,16,512]{2,0,1:T(8,128)} %bitcast.289), calls=%async_computation.1 | async-start | bytes 2097152 | tf_op jit(solution)/shard_map/all_to_all | solution.py:113
  75.5 11.5 %all-to-all-start.7 = ((bf16[512,4,128]{2,0,1:T(8,128)(2,1)}), bf16[512,4,128]{2,0,1:T(8,128)(2,1)S(1)}, u32[]{:S(2)}, u32[]{:S(2)}) async-start(bf16[512,4,128]{2,0,1:T(8,128)(2,1)} %copy.229), calls=%async_computation.7 | async-start | bytes 1048576 | tf_op jit(solution)/shard_map/all_to_all | solution.py:134
  87.0 14.4 %all-to-all-start.2 = ((f32[512,4,128]{2,0,1:T(8,128)}), f32[512,4,128]{2,0,1:T(8,128)S(1)}, u32[]{:S(2)}, u32[]{:S(2)}) async-start(f32[512,4,128]{2,0,1:T(8,128)} %copy.197), calls=%async_computation.2 | async-start | bytes 2097152 | tf_op jit(solution)/shard_map/all_to_all | solution.py:112
  90.5 154.7 %all-reduce.4.cloned.1.call-start = ((), (), s32[]{:S(2)}) async-start(), calls=%async_computation.12 | async-start | bytes 1048576 | tf_op jit(solution)/shard_map/psum | solution.py:180
  180.9 7.9 %copy-start.4 = (f32[32,128,128]{2,0,1:T(8,128)S(1)}, f32[32,128,128]{2,0,1:T(8,128)}, u32[]{:S(2)}) copy-start(f32[32,128,128]{2,0,1:T(8,128)} %fusion.34) | copy-start | bytes 6291460
  199.7 22.4 %all-to-all-start.4 = ((bf16[4,512,128]{2,1,0:T(8,128)(2,1)}), bf16[4,512,128]{2,1,0:T(8,128)(2,1)}, u32[]{:S(2)}, u32[]{:S(2)}) async-start(bf16[4,512,128]{2,1,0:T(8,128)(2,1)} %bitcast.306), calls=%async_computation.4 | async-start | bytes 1048576 | tf_op jit(solution)/shard_map/all_to_all | solution.py:129
  222.1 13.3 %all-to-all-start.8 = ((bf16[4,512,128]{2,1,0:T(8,128)(2,1)}), bf16[4,512,128]{2,1,0:T(8,128)(2,1)}, u32[]{:S(2)}, u32[]{:S(2)}) async-start(bf16[4,512,128]{2,1,0:T(8,128)(2,1)} %bitcast.38), calls=%async_computation.8 | async-start | bytes 1048576 | tf_op jit(solution)/shard_map/all_to_all | solution.py:146
  235.4 13.7 %all-to-all-start.5 = ((bf16[16,32,512]{2,1,0:T(8,128)(2,1)}), bf16[16,32,512]{2,1,0:T(8,128)(2,1)S(1)}, u32[]{:S(2)}, u32[]{:S(2)}) async-start(bf16[16,32,512]{2,1,0:T(8,128)(2,1)} %convert_element_type.345), calls=%async_computation.5 | async-start | bytes 1048576 | tf_op jit(solution)/shard_map/all_to_all | solution.py:152
  243.5 10.4 %copy-start.19 = (bf16[512,2,256]{2,1,0:T(2,128)(2,1)S(1)}, bf16[512,2,256]{2,1,0:T(2,128)(2,1)}, u32[]{:S(2)}) copy-start(bf16[512,2,256]{2,1,0:T(2,128)(2,1)} %reshape.179) | copy-start | bytes 1572868
  243.5 12.4 %copy-start.12 = (bf16[512,2,256]{2,1,0:T(2,128)(2,1)S(1)}, bf16[512,2,256]{2,1,0:T(2,128)(2,1)}, u32[]{:S(2)}) copy-start(bf16[512,2,256]{2,1,0:T(2,128)(2,1)} %copy-done.11) | copy-start | bytes 1572868
  243.5 12.4 %copy-start.21 = (bf16[512,2,256]{0,2,1:T(8,128)(2,1)S(1)}, bf16[512,2,256]{0,2,1:T(8,128)(2,1)}, u32[]{:S(2)}) copy-start(bf16[512,2,256]{0,2,1:T(8,128)(2,1)} %copy-done.20) | copy-start | bytes 1572868
  249.1 12.9 %all-to-all-start.10 = ((bf16[4,512,128]{2,1,0:T(8,128)(2,1)}), bf16[4,512,128]{2,1,0:T(8,128)(2,1)S(1)}, u32[]{:S(2)}, u32[]{:S(2)}) async-start(bf16[4,512,128]{2,1,0:T(8,128)(2,1)} %all-reduce.4.cloned.1.call-done), calls=%async_computation.10 | async-start | bytes 1048576 | tf_op jit(solution)/shard_map/all_to_all | solution.py:182
  255.9 11.7 %copy-start.23 = (bf16[512,2,256]{0,2,1:T(8,128)(2,1)S(1)}, bf16[512,2,256]{0,2,1:T(8,128)(2,1)}, u32[]{:S(2)}) copy-start(bf16[512,2,256]{0,2,1:T(8,128)(2,1)} %copy-done.22) | copy-start | bytes 1572868
  262.0 14.9 %all-to-all-start.9 = ((bf16[16,32,512]{2,1,0:T(8,128)(2,1)}), bf16[16,32,512]{2,1,0:T(8,128)(2,1)S(1)}, u32[]{:S(2)}, u32[]{:S(2)}) async-start(bf16[16,32,512]{2,1,0:T(8,128)(2,1)} %convert_element_type.362), calls=%async_computation.9 | async-start | bytes 1048576 | tf_op jit(solution)/shard_map/all_to_all | solution.py:190
  265.5 66.4 %all-reduce.6.cloned.1.call-start = ((), (), s32[]{:S(2)}) async-start(), calls=%async_computation.13 | async-start | bytes 2097152 | tf_op jit(solution)/shard_map/psum | solution.py:164
  276.9 61.6 %all-to-all-start.11 = ((bf16[16,32,512]{2,1,0:T(8,128)(2,1)}), bf16[16,32,512]{2,1,0:T(8,128)(2,1)S(1)}, u32[]{:S(2)}, u32[]{:S(2)}) async-start(bf16[16,32,512]{2,1,0:T(8,128)(2,1)} %all_to_all.151), calls=%async_computation.11 | async-start | bytes 1048576 | tf_op jit(solution)/shard_map/all_to_all | solution.py:181
  (27 other events, 100.1 us)
Sparse Core Ops, SparseCore 0:
  181.0 19.7 all-reduce.3
Sparse Core Ops, SparseCore 1:
  269.2 62.6 all-reduce.5
where the time goes:
time: 353 us; the launch traced here: 347 us
  matrix products  131 us (37%)
  waiting for transfers between devices  106 us (30%)
  starting transfers between devices  51.5 us (15%)
  local copies, waits for them, and re-layouts  34.6 us (10%)
  between operations  16.5 us (5%)
  other arithmetic  7.54 us (2%)
    dot_general x12, matrix products, across_first(): jnp.einsum('kn,nmc->kmc', matrix, array, precision=table_mode, preferred_...  62.6 us
    dot_general x24, matrix products, across_second(): jnp.einsum('kmc,ml->klc', array, matrix, precision=table_mode, preferred_...  56.2 us
    psum x1, waiting for transfers between devices, shards(): lax.psum((weight_term(inputs, query_back, blocks) * factor).astype(jnp.bf...  48.8 us
    unnamed x79, local copies, waits for them, and re-layouts  10.9 us
    all_to_all x1, waiting for transfers between devices, shards(): lax.all_to_all(tokens[0], 'tensor', split_axis=1, concat_axis=0, tiled=True)  10.2 us
    all_to_all x1, waiting for transfers between devices, shards(): lax.all_to_all(filter_taps, 'tensor', split_axis=1, concat_axis=0, tiled=...  9.66 us
    all_to_all x1, starting transfers between devices, shards(): lax.all_to_all(tokens[0], 'tensor', split_axis=1, concat_axis=0, tiled=True)  7.15 us
  transfers between devices with their start and end apart: 14, of which 10 were waited for; matrix products, arithmetic and copies ran while one was open for 24% of the time, Pallas kernels for 0%

commit v1 on v0

--- a/solution.py
+++ b/solution.py
@@ -96,6 +96,79 @@
     return signal.reshape(half * cosine_second.shape[0], -1)
 
 
+def spectral_tables(length):
+    first = 128
+    second = length // first
+    half = first // 2
+    cosine_first, sine_first = angle_table(first, first, first)
+    cosine_second, sine_second = angle_table(second, second, second)
+    cosine_twist, sine_twist = angle_table(first, second, length)
+    forward_first = jnp.concatenate([cosine_first[:, :half], -sine_first[:, :half]], axis=0)
+    forward_second = jnp.stack(
+        [
+            jnp.stack([cosine_second, -sine_second], axis=1),
+            jnp.stack([sine_second, cosine_second], axis=1),
+        ]
+    )
+    inverse_second = jnp.stack(
+        [
+            jnp.stack([cosine_second, sine_second], axis=1),
+            jnp.stack([-sine_second, cosine_second], axis=1),
+        ]
+    )
+    inverse_first = jnp.stack([cosine_first[:half], -sine_first[:half]], axis=1) / length
+    return (
+        forward_first,
+        forward_second,
+        inverse_second,
+        inverse_first,
+        cosine_twist[:, :, None],
+        sine_twist[:, :, None],
+    )
+
+
+def spectra(signal, tables):
+    forward_first, forward_second, _, _, cosine_twist, sine_twist = tables
+    first = cosine_twist.shape[0]
+    half = first // 2
+    shaped = signal.reshape(half, cosine_twist.shape[1], signal.shape[1])
+    section = jnp.einsum(
+        "kn,nmc->kmc", forward_first, shaped, precision=table_mode,
+        preferred_element_type=jnp.float32,
+    )
+    real_section, imag_section = section[:first], section[first:]
+    turned = jnp.stack(
+        [
+            real_section * cosine_twist + imag_section * sine_twist,
+            imag_section * cosine_twist - real_section * sine_twist,
+        ]
+    )
+    return jnp.einsum(
+        "rkmc,rmsl->sklc", turned, forward_second, precision=table_mode,
+        preferred_element_type=jnp.float32,
+    )
+
+
+def signals(spec, tables):
+    _, _, inverse_second, inverse_first, cosine_twist, sine_twist = tables
+    section = jnp.einsum(
+        "sklc,slrm->rkmc", spec, inverse_second, precision=table_mode,
+        preferred_element_type=jnp.float32,
+    )
+    real_section, imag_section = section[0], section[1]
+    turned = jnp.stack(
+        [
+            real_section * cosine_twist - imag_section * sine_twist,
+            imag_section * cosine_twist + real_section * sine_twist,
+        ]
+    )
+    out = jnp.einsum(
+        "nrk,rkmc->nmc", inverse_first, turned, precision=table_mode,
+        preferred_element_type=jnp.float32,
+    )
+    return out.reshape(-1, out.shape[-1])
+
+
 def shards(
     tokens, filter_taps, query_weight, key_weight, value_weight, output_weight, out_cotangent
 ):
@@ -117,31 +190,51 @@
         tiled=True,
     )
     length = taps.shape[0]
-    tables = make_tables(2 * length)
+    width = taps.shape[1]
+    tables = spectral_tables(2 * length)
     gated_time = lax.all_to_all(gated, "context", split_axis=1, concat_axis=0, tiled=True)
-    real_taps, imag_taps = forward_transform(taps, tables)
-    real_gated, imag_gated = forward_transform(gated_time.astype(jnp.float32), tables)
-    conv_time = inverse_transform(
-        real_taps * real_gated - imag_taps * imag_gated,
-        real_taps * imag_gated + imag_taps * real_gated,
-        tables,
-    )
-    conv = lax.all_to_all(
-        conv_time.astype(jnp.bfloat16), "context", split_axis=0, concat_axis=1, tiled=True
-    )
     back_weighted = blockwise_back(upstream, output_weight)
     conv_grad = (back_weighted * query_wide).astype(jnp.bfloat16)
     grad_time = lax.all_to_all(conv_grad, "context", split_axis=1, concat_axis=0, tiled=True)
-    real_grad, imag_grad = forward_transform(grad_time.astype(jnp.float32), tables)
-    gated_time_back = inverse_transform(
-        real_taps * real_grad + imag_taps * imag_grad,
-        real_taps * imag_grad - imag_taps * real_grad,
+    spec = spectra(
+        jnp.concatenate(
+            [taps, gated_time.astype(jnp.float32), grad_time.astype(jnp.float32)], axis=1
+        ),
         tables,
     )
-    taps_back = inverse_transform(
-        real_grad * real_gated + imag_grad * imag_gated,
-        imag_grad * real_gated - real_grad * imag_gated,
-        tables,
+    real_spec, imag_spec = spec[0], spec[1]
+    real_taps, real_gated, real_grad = (
+        real_spec[..., :width], real_spec[..., width : 2 * width], real_spec[..., 2 * width :]
+    )
+    imag_taps, imag_gated, imag_grad = (
+        imag_spec[..., :width], imag_spec[..., width : 2 * width], imag_spec[..., 2 * width :]
+    )
+    products = jnp.stack(
+        [
+            jnp.concatenate(
+                [
+                    real_taps * real_gated - imag_taps * imag_gated,
+                    real_taps * real_grad + imag_taps * imag_grad,
+                    real_grad * real_gated + imag_grad * imag_gated,
+                ],
+                axis=-1,
+            ),
+            jnp.concatenate(
+                [
+                    real_taps * imag_gated + imag_taps * real_gated,
+                    real_taps * imag_grad - imag_taps * real_grad,
+                    imag_grad * real_gated - real_grad * imag_gated,
+                ],
+                axis=-1,
+            ),
+        ]
+    )
+    results = signals(products, tables)
+    conv_time = results[:, :width]
+    gated_time_back = results[:, width : 2 * width]
+    taps_back = results[:, 2 * width :]
+    conv = lax.all_to_all(
+        conv_time.astype(jnp.bfloat16), "context", split_axis=0, concat_axis=1, tiled=True
     )
     gated_narrow = lax.all_to_all(
         gated_time_back.astype(jnp.bfloat16), "context", split_axis=0, concat_axis=1, tiled=True

time: 353 us -> 347 us (0.983)
  matrix products: 131 us -> 59 us
  other arithmetic: 7.54 us -> 51.7 us
  local copies, waits for them, and re-layouts: 34.6 us -> 45.9 us
  waiting for transfers between devices: 106 us -> 116 us
    dot_general x36 -> x4, matrix products: 119 us -> 43.9 us  [the longest x1 20.8 us: spectra(): jnp.einsum('rkmc,rmsl->sklc', turned, forward_second, precision=table_mod...]
    another operation x0 -> x8, other arithmetic: none -> 26.3 us  [the longest x2 12.2 us: spectra(): jnp.stack([real_section * cosine_twist + imag_section * sine_twist, imag_...]
    sub x0 -> x2, other arithmetic: none -> 11.7 us  [the longest x1 7.92 us: shards(): real_taps * real_gated - imag_taps * imag_gated]
    squeeze x0 -> x1, local copies, waits for them, and re-layouts: none -> 8.55 us  [shards(): real_spec, imag_spec = (spec[0], spec[1])]
    all_to_all x1, waiting for transfers between devices: 0.01 us -> 7.41 us  [shards(): lax.all_to_all(conv_time.astype(jnp.bfloat16), 'context', split_axis=0, c...]
    unnamed x79 -> x71, local copies, waits for them, and re-layouts: 10.9 us -> 12.8 us
  transfers between devices with their start and end apart: 14 -> 14, of which waited for: 10 -> 11; matrix products, arithmetic and copies ran while one was open for 24% -> 15% of each run, Pallas kernels for 0% -> 0%
where the time goes in v1:
time: 347 us; the launch traced here: 341 us
  waiting for transfers between devices  116 us (33%)
  matrix products  59 us (17%)
  starting transfers between devices  52.3 us (15%)
  other arithmetic  51.7 us (15%)
  local copies, waits for them, and re-layouts  45.9 us (13%)
  between operations  16.3 us (5%)
    psum x1, waiting for transfers between devices, shards(): lax.psum((weight_term(inputs, query_back, blocks) * factor).astype(jnp.bf...  47.9 us
    dot_general x1, matrix products, spectra(): jnp.einsum('rkmc,rmsl->sklc', turned, forward_second, precision=table_mod...  20.8 us
    unnamed x71, local copies, waits for them, and re-layouts  12.8 us
    dot_general x1, matrix products, signals(): jnp.einsum('nrk,rkmc->nmc', inverse_first, turned, precision=table_mode,...  12.3 us
    another operation x2, other arithmetic, spectra(): jnp.stack([real_section * cosine_twist + imag_section * sine_twist, imag_...  12.2 us
    all_to_all x1, waiting for transfers between devices, shards(): lax.all_to_all(filter_taps, 'tensor', split_axis=1, concat_axis=0, tiled=...  11.7 us
    all_to_all x1, waiting for transfers between devices, shards(): lax.all_to_all(out_cotangent[0], 'tensor', split_axis=1, concat_axis=0, t...  10.3 us
    all_to_all x1, waiting for transfers between devices, shards(): lax.all_to_all(tokens[0], 'tensor', split_axis=1, concat_axis=0, tiled=True)  9.24 us
  transfers between devices with their start and end apart: 14, of which 11 were waited for; matrix products, arithmetic and copies ran while one was open for 15% of the time, Pallas kernels for 0%

profile of v1, /device:TPU:0, one launch (start us, length us, event | category | flops | bytes accessed | tf_op | source)
XLA Modules:
  0.0 341.0 jit_solution(5098047560574592954)
XLA Ops:
  10.4 7.1 %all-to-all-start = ((bf16[32,16,512]{2,0,1:T(8,128)(2,1)}), bf16[32,16,512]{2,0,1:T(8,128)(2,1)S(1)}, u32[]{:S(2)}, u32[]{:S(2)}) async-start(bf16[32,16,512]{2,0,1:T(8,128)(2,1)} %copy.161), calls=%async_computation | async-start | bytes 1048576 | tf_op jit(solution)/shard_map/all_to_all | solution.py:176
  19.8 9.2 %all-to-all-done = bf16[32,16,512]{2,0,1:T(8,128)(2,1)S(1)} async-done(((bf16[32,16,512]{2,0,1:T(8,128)(2,1)}), bf16[32,16,512]{2,0,1:T(8,128)(2,1)S(1)}, u32[]{:S(2)}, u32[]{:S(2)}) %all-to-all-start) | async-done | bytes 524320 | tf_op jit(solution)/shard_map/all_to_all | solution.py:176
  32.8 10.3 %all-to-all-done.4 = bf16[32,16,512]{2,0,1:T(8,128)(2,1)S(1)} async-done(((bf16[32,16,512]{2,0,1:T(8,128)(2,1)}), bf16[32,16,512]{2,0,1:T(8,128)(2,1)S(1)}, u32[]{:S(2)}, u32[]{:S(2)}) %all-to-all-start.4) | async-done | bytes 524320 | tf_op jit(solution)/shard_map/all_to_all | solution.py:177
  46.9 5.3 %all-to-all-start.5 = ((bf16[512,4,128]{2,0,1:T(8,128)(2,1)}), bf16[512,4,128]{2,0,1:T(8,128)(2,1)S(1)}, u32[]{:S(2)}, u32[]{:S(2)}) async-start(bf16[512,4,128]{2,0,1:T(8,128)(2,1)} %copy.174), calls=%async_computation.5 | async-start | bytes 1048576 | tf_op jit(solution)/shard_map/all_to_all | solution.py:198
  54.5 5.7 %all-to-all-done.5 = bf16[512,4,128]{2,0,1:T(8,128)(2,1)S(1)} async-done(((bf16[512,4,128]{2,0,1:T(8,128)(2,1)}), bf16[512,4,128]{2,0,1:T(8,128)(2,1)S(1)}, u32[]{:S(2)}, u32[]{:S(2)}) %all-to-all-start.5) | async-done | bytes 524320 | tf_op jit(solution)/shard_map/all_to_all | solution.py:198
  66.4 11.7 %all-to-all-done.1 = f32[32,16,512]{2,0,1:T(8,128)S(1)} async-done(((f32[32,16,512]{2,0,1:T(8,128)}), f32[32,16,512]{2,0,1:T(8,128)S(1)}, u32[]{:S(2)}, u32[]{:S(2)}) %all-to-all-start.1) | async-done | bytes 1048608 | tf_op jit(solution)/shard_map/all_to_all | solution.py:186
  85.7 4.1 %all-to-all-done.3 = bf16[512,4,128]{2,0,1:T(8,128)(2,1)S(1)} async-done(((bf16[512,4,128]{2,0,1:T(8,128)(2,1)}), bf16[512,4,128]{2,0,1:T(8,128)(2,1)S(1)}, u32[]{:S(2)}, u32[]{:S(2)}) %all-to-all-start.3) | async-done | bytes 524320 | tf_op jit(solution)/shard_map/all_to_all | solution.py:195
  99.8 5.3 %all-to-all-done.2 = f32[512,4,128]{2,0,1:T(8,128)S(1)} async-done(((f32[512,4,128]{2,0,1:T(8,128)}), f32[512,4,128]{2,0,1:T(8,128)S(1)}, u32[]{:S(2)}, u32[]{:S(2)}) %all-to-all-start.2) | async-done | bytes 1048608 | tf_op jit(solution)/shard_map/all_to_all | solution.py:185
  105.8 5.2 %fusion.14 = f32[256,32,384]{2,0,1:T(8,128)S(1)} fusion(f32[64,32,128]{2,0,1:T(8,128)S(1)} %copy.177, f32[64,32,128]{2,0,1:T(8,128)S(1)} %copy.176, f32[64,32,128]{2,0,1:T(8,128)S(1)} %copy.175, f32[128,64]{1,0:T(8,128)S(1)} %copy-done.24, f32[128,64]{1,0:T(8,128)S(1)} %bitcast.183), kind=kOutput, calls=%fused_computation.21 | convolution fusion | flops 1209548800 | bytes 15794176 | tf_op jit(solution)/shard_map/kn,nmc->kmc/dot_general | solution.py:135
  114.7 8.5 %pad_maximum_fusion = f32[2,128,32,384]{3,1,2,0:T(8,128)} fusion(f32[1,128,32,384]{3,1,2,0:T(8,128)} %get-tuple-element.49, f32[1,128,32,384]{3,1,2,0:T(8,128)S(1)} %get-tuple-element.48), kind=kLoop, calls=%fused_computation | loop fusion | flops 3145728 | bytes 25165824 | tf_op jit(solution)/shard_map/stack | solution.py:140
  123.2 20.8 %fusion.8 = f32[2,128,32,384]{3,2,1,0:T(8,128)} fusion(f32[2,128,32,384]{3,1,2,0:T(8,128)} %pad_maximum_fusion, f32[1,32,2,32]{1,3,0,2:T(8,128)S(1)} %copy-done.31, f32[1,32,2,32]{1,3,0,2:T(8,128)S(1)} %copy-done.32), kind=kOutput, calls=%fused_computation.19 | convolution fusion | flops 1207963648 | bytes 25182208 | tf_op jit(solution)/shard_map/rkmc,rmsl->sklc/dot_general | solution.py:146
  144.0 8.6 %slice_bitcast_fusion.1 = (f32[128,32,384]{2,1,0:T(8,128)S(1)}, f32[128,32,384]{2,1,0:T(8,128)}) fusion(f32[2,128,32,384]{3,2,1,0:T(8,128)} %fusion.8), kind=kLoop, calls=%fused_computation.12 | loop fusion | bytes 25165824 | tf_op jit(solution)/shard_map/squeeze | solution.py:205
  152.5 7.9 %multiply_subtract_fusion.3 = (f32[128,32,128]{2,1,0:T(8,128)}, f32[128,32,128]{2,1,0:T(8,128)}, f32[128,32,128]{2,1,0:T(8,128)}, f32[128,32,128]{2,1,0:T(8,128)}) fusion(f32[128,32,384]{2,1,0:T(8,128)} %get-tuple-element.57, f32[128,32,384]{2,1,0:T(8,128)S(1)} %get-tuple-element.56), kind=kLoop, calls=%fused_computation.32 | loop fusion | flops 6291456 | bytes 20971520 | tf_op jit(solution)/shard_map/sub | solution.py:216
  167.1 5.6 %fusion.11 = f32[2,128,32,384]{3,2,1,0:T(8,128)S(1)} fusion(f32[1,128,32,384]{3,2,1,0:T(8,128)S(1)} %maximum_bitcast_fusion.1, f32[1,128,32,384]{3,2,1,0:T(8,128)S(1)} %maximum_bitcast_fusion, f32[1,32,2,32]{1,3,2,0:T(8,128)S(1)} %copy-done.30, f32[1,32,2,32]{1,3,2,0:T(8,128)S(1)} %copy-done.29), kind=kOutput, calls=%fused_computation.20 | convolution fusion | flops 1211109376 | bytes 25182208 | tf_op jit(solution)/shard_map/sklc,slrm->rkmc/dot_general | solution.py:154
  176.6 8.7 %pad_maximum_fusion.2 = f32[2,128,32,384]{3,2,1,0:T(8,128)} fusion(f32[1,128,32,384]{3,2,1,0:T(8,128)} %get-tuple-element.47, f32[1,128,32,384]{3,2,1,0:T(8,128)S(1)} %get-tuple-element.46), kind=kLoop, calls=%fused_computation.2 | loop fusion | flops 3145728 | bytes 25165824 | tf_op jit(solution)/shard_map/stack | solution.py:159
  185.3 12.3 %fusion.20 = f32[64,32,384]{2,0,1:T(8,128)S(1)} fusion(f32[2,128,32,384]{3,2,1,0:T(8,128)} %pad_maximum_fusion.2, f32[64,1,128]{2,0,1:T(8,128)S(1)} %copy-done.27, f32[64,1,128]{2,0,1:T(8,128)S(1)} %copy-done.28), kind=kOutput, calls=%fused_computation.33 | convolution fusion | flops 1207992320 | bytes 15794176 | tf_op jit(solution)/shard_map/nrk,rkmc->nmc/dot_general | solution.py:165
  200.6 4.1 %all-to-all-start.6 = ((bf16[4,512,128]{2,1,0:T(8,128)(2,1)}), bf16[4,512,128]{2,1,0:T(8,128)(2,1)}, u32[]{:S(2)}, u32[]{:S(2)}) async-start(bf16[4,512,128]{2,1,0:T(8,128)(2,1)} %bitcast.176), calls=%async_computation.6 | async-start | bytes 1048576 | tf_op jit(solution)/shard_map/all_to_all | solution.py:236
  205.7 7.4 %all-to-all-done.6 = bf16[4,512,128]{2,1,0:T(8,128)(2,1)} async-done(((bf16[4,512,128]{2,1,0:T(8,128)(2,1)}), bf16[4,512,128]{2,1,0:T(8,128)(2,1)}, u32[]{:S(2)}, u32[]{:S(2)}) %all-to-all-start.6) | async-done | bytes 524320 | tf_op jit(solution)/shard_map/all_to_all | solution.py:236
  225.9 4.5 %all-to-all-start.7 = ((bf16[16,32,512]{2,1,0:T(8,128)(2,1)}), bf16[16,32,512]{2,1,0:T(8,128)(2,1)}, u32[]{:S(2)}, u32[]{:S(2)}) async-start(bf16[16,32,512]{2,1,0:T(8,128)(2,1)} %convert_element_type.289), calls=%async_computation.7 | async-start | bytes 1048576 | tf_op jit(solution)/shard_map/all_to_all | solution.py:245
  240.6 4.8 %all-to-all-start.10 = ((bf16[4,512,128]{2,1,0:T(8,128)(2,1)}), bf16[4,512,128]{2,1,0:T(8,128)(2,1)S(1)}, u32[]{:S(2)}, u32[]{:S(2)}) async-start(bf16[4,512,128]{2,1,0:T(8,128)(2,1)} %all-reduce.4.cloned.1.call-done), calls=%async_computation.10 | async-start | bytes 1048576 | tf_op jit(solution)/shard_map/all_to_all | solution.py:275
  248.4 5.0 %all-to-all-done.10 = bf16[4,512,128]{2,1,0:T(8,128)(2,1)S(1)} async-done(((bf16[4,512,128]{2,1,0:T(8,128)(2,1)}), bf16[4,512,128]{2,1,0:T(8,128)(2,1)S(1)}, u32[]{:S(2)}, u32[]{:S(2)}) %all-to-all-start.10) | async-done | bytes 524320 | tf_op jit(solution)/shard_map/all_to_all | solution.py:275
  253.4 4.9 %all-to-all-start.9 = ((bf16[16,32,512]{2,1,0:T(8,128)(2,1)}), bf16[16,32,512]{2,1,0:T(8,128)(2,1)S(1)}, u32[]{:S(2)}, u32[]{:S(2)}) async-start(bf16[16,32,512]{2,1,0:T(8,128)(2,1)} %convert_element_type.302), calls=%async_computation.9 | async-start | bytes 1048576 | tf_op jit(solution)/shard_map/all_to_all | solution.py:283
  262.8 6.7 %all-to-all-done.9 = bf16[16,32,512]{2,1,0:T(8,128)(2,1)S(1)} async-done(((bf16[16,32,512]{2,1,0:T(8,128)(2,1)}), bf16[16,32,512]{2,1,0:T(8,128)(2,1)S(1)}, u32[]{:S(2)}, u32[]{:S(2)}) %all-to-all-start.9) | async-done | bytes 524320 | tf_op jit(solution)/shard_map/all_to_all | solution.py:283
  276.8 47.9 %all-reduce.6.cloned.1.call-done = (bf16[2,256,256]{1,2,0:T(8,128)(2,1)}, bf16[2,256,256]{1,2,0:T(8,128)(2,1)}, bf16[2,256,256]{1,2,0:T(8,128)(2,1)}, bf16[2,256,256]{2,1,0:T(8,128)(2,1)}) async-done(((bf16[2,256,256]{1,2,0:T(8,128)(2,1)}, bf16[2,256,256]{1,2,0:T(8,128)(2,1)}, bf16[2,256,256]{1,2,0:T(8,128)(2,1)}, bf16[2,256,256]{2,1,0:T(8,128)(2,1)}), (bf16[2,256,256]{1,2,0:T(8,128)(2,1)}, ...) | async-done | bytes 1048592 | tf_op jit(solution)/shard_map/psum | solution.py:257
  (149 shorter events, 103.0 us)
Async XLA Ops:
  8.0 36.6 %copy-start = (bf16[2,256,256]{2,1,0:T(8,128)(2,1)S(1)}, bf16[2,256,256]{2,1,0:T(8,128)(2,1)}, u32[]{:S(2)}) copy-start(bf16[2,256,256]{2,1,0:T(8,128)(2,1)} %param.12) | copy-start | bytes 786436
  8.0 35.2 %copy-start.19 = (bf16[2,256,256]{2,1,0:T(8,128)(2,1)S(1)}, bf16[2,256,256]{2,1,0:T(8,128)(2,1)}, u32[]{:S(2)}) copy-start(bf16[2,256,256]{2,1,0:T(8,128)(2,1)} %param.9) | copy-start | bytes 786436
  10.4 18.7 %all-to-all-start = ((bf16[32,16,512]{2,0,1:T(8,128)(2,1)}), bf16[32,16,512]{2,0,1:T(8,128)(2,1)S(1)}, u32[]{:S(2)}, u32[]{:S(2)}) async-start(bf16[32,16,512]{2,0,1:T(8,128)(2,1)} %copy.161), calls=%async_computation | async-start | bytes 1048576 | tf_op jit(solution)/shard_map/all_to_all | solution.py:176
  29.1 14.0 %all-to-all-start.4 = ((bf16[32,16,512]{2,0,1:T(8,128)(2,1)}), bf16[32,16,512]{2,0,1:T(8,128)(2,1)S(1)}, u32[]{:S(2)}, u32[]{:S(2)}) async-start(bf16[32,16,512]{2,0,1:T(8,128)(2,1)} %copy.172), calls=%async_computation.4 | async-start | bytes 1048576 | tf_op jit(solution)/shard_map/all_to_all | solution.py:177
  32.8 31.5 %copy-start.7 = (bf16[512,2,256]{2,1,0:T(2,128)(2,1)}, bf16[512,2,256]{2,1,0:T(2,128)(2,1)S(1)}, u32[]{:S(2)}) copy-start(bf16[512,2,256]{2,1,0:T(2,128)(2,1)S(1)} %reshape.243) | copy-start | bytes 1572868
  43.1 20.8 %copy-start.21 = (bf16[2,256,256]{2,1,0:T(8,128)(2,1)S(1)}, bf16[2,256,256]{2,1,0:T(8,128)(2,1)}, u32[]{:S(2)}) copy-start(bf16[2,256,256]{2,1,0:T(8,128)(2,1)} %param.10) | copy-start | bytes 786436
  43.2 17.0 %copy-start.13 = (bf16[512,2,256]{2,1,0:T(2,128)(2,1)}, bf16[512,2,256]{2,1,0:T(2,128)(2,1)S(1)}, u32[]{:S(2)}) copy-start(bf16[512,2,256]{2,1,0:T(2,128)(2,1)S(1)} %reshape.244) | copy-start | bytes 1572868
  43.2 21.1 %copy-start.20 = (bf16[2,256,256]{2,1,0:T(8,128)(2,1)S(1)}, bf16[2,256,256]{2,1,0:T(8,128)(2,1)}, u32[]{:S(2)}) copy-start(bf16[2,256,256]{2,1,0:T(8,128)(2,1)} %param.11) | copy-start | bytes 786436
  46.9 13.4 %all-to-all-start.5 = ((bf16[512,4,128]{2,0,1:T(8,128)(2,1)}), bf16[512,4,128]{2,0,1:T(8,128)(2,1)S(1)}, u32[]{:S(2)}, u32[]{:S(2)}) async-start(bf16[512,4,128]{2,0,1:T(8,128)(2,1)} %copy.174), calls=%async_computation.5 | async-start | bytes 1048576 | tf_op jit(solution)/shard_map/all_to_all | solution.py:198
  60.2 17.9 %all-to-all-start.1 = ((f32[32,16,512]{2,0,1:T(8,128)}), f32[32,16,512]{2,0,1:T(8,128)S(1)}, u32[]{:S(2)}, u32[]{:S(2)}) async-start(f32[32,16,512]{2,0,1:T(8,128)} %bitcast.157), calls=%async_computation.1 | async-start | bytes 2097152 | tf_op jit(solution)/shard_map/all_to_all | solution.py:186
  78.2 11.5 %all-to-all-start.3 = ((bf16[512,4,128]{2,0,1:T(8,128)(2,1)}), bf16[512,4,128]{2,0,1:T(8,128)(2,1)S(1)}, u32[]{:S(2)}, u32[]{:S(2)}) async-start(bf16[512,4,128]{2,0,1:T(8,128)(2,1)} %copy.171), calls=%async_computation.3 | async-start | bytes 1048576 | tf_op jit(solution)/shard_map/all_to_all | solution.py:195
  90.5 14.6 %all-to-all-start.2 = ((f32[512,4,128]{2,0,1:T(8,128)}), f32[512,4,128]{2,0,1:T(8,128)S(1)}, u32[]{:S(2)}, u32[]{:S(2)}) async-start(f32[512,4,128]{2,0,1:T(8,128)} %copy.166), calls=%async_computation.2 | async-start | bytes 2097152 | tf_op jit(solution)/shard_map/all_to_all | solution.py:185
  200.6 12.5 %all-to-all-start.6 = ((bf16[4,512,128]{2,1,0:T(8,128)(2,1)}), bf16[4,512,128]{2,1,0:T(8,128)(2,1)}, u32[]{:S(2)}, u32[]{:S(2)}) async-start(bf16[4,512,128]{2,1,0:T(8,128)(2,1)} %bitcast.176), calls=%async_computation.6 | async-start | bytes 1048576 | tf_op jit(solution)/shard_map/all_to_all | solution.py:236
  204.7 33.5 %all-reduce.4.cloned.1.call-start = ((), (), s32[]{:S(2)}) async-start(), calls=%async_computation.12 | async-start | bytes 1048576 | tf_op jit(solution)/shard_map/psum | solution.py:273
  213.1 12.1 %all-to-all-start.8 = ((bf16[4,512,128]{2,1,0:T(8,128)(2,1)}), bf16[4,512,128]{2,1,0:T(8,128)(2,1)S(1)}, u32[]{:S(2)}, u32[]{:S(2)}) async-start(bf16[4,512,128]{2,1,0:T(8,128)(2,1)} %bitcast.175), calls=%async_computation.8 | async-start | bytes 1048576 | tf_op jit(solution)/shard_map/all_to_all | solution.py:239
  218.0 13.9 %copy-start.10 = (bf16[2,256,512]{2,1,0:T(8,128)(2,1)S(1)}, bf16[2,256,512]{2,1,0:T(8,128)(2,1)}, u32[]{:S(2)}) copy-start(bf16[2,256,512]{2,1,0:T(8,128)(2,1)} %copy-done.9) | copy-start | bytes 1572868
  225.9 14.6 %all-to-all-start.7 = ((bf16[16,32,512]{2,1,0:T(8,128)(2,1)}), bf16[16,32,512]{2,1,0:T(8,128)(2,1)}, u32[]{:S(2)}, u32[]{:S(2)}) async-start(bf16[16,32,512]{2,1,0:T(8,128)(2,1)} %convert_element_type.289), calls=%async_computation.7 | async-start | bytes 1048576 | tf_op jit(solution)/shard_map/all_to_all | solution.py:245
  231.9 13.4 %copy-start.8 = (bf16[512,2,256]{2,1,0:T(2,128)(2,1)S(1)}, bf16[512,2,256]{2,1,0:T(2,128)(2,1)}, u32[]{:S(2)}) copy-start(bf16[512,2,256]{2,1,0:T(2,128)(2,1)} %copy-done.7) | copy-start | bytes 1572868
  231.9 13.4 %copy-start.16 = (bf16[512,2,256]{0,2,1:T(8,128)(2,1)S(1)}, bf16[512,2,256]{0,2,1:T(8,128)(2,1)}, u32[]{:S(2)}) copy-start(bf16[512,2,256]{0,2,1:T(8,128)(2,1)} %copy-done.15) | copy-start | bytes 1572868
  235.1 24.2 %copy-start.14 = (bf16[512,2,256]{2,1,0:T(2,128)(2,1)S(1)}, bf16[512,2,256]{2,1,0:T(2,128)(2,1)}, u32[]{:S(2)}) copy-start(bf16[512,2,256]{2,1,0:T(2,128)(2,1)} %copy-done.13) | copy-start | bytes 1572868
  240.6 12.8 %all-to-all-start.10 = ((bf16[4,512,128]{2,1,0:T(8,128)(2,1)}), bf16[4,512,128]{2,1,0:T(8,128)(2,1)S(1)}, u32[]{:S(2)}, u32[]{:S(2)}) async-start(bf16[4,512,128]{2,1,0:T(8,128)(2,1)} %all-reduce.4.cloned.1.call-done), calls=%async_computation.10 | async-start | bytes 1048576 | tf_op jit(solution)/shard_map/all_to_all | solution.py:275
  253.4 16.2 %all-to-all-start.9 = ((bf16[16,32,512]{2,1,0:T(8,128)(2,1)}), bf16[16,32,512]{2,1,0:T(8,128)(2,1)S(1)}, u32[]{:S(2)}, u32[]{:S(2)}) async-start(bf16[16,32,512]{2,1,0:T(8,128)(2,1)} %convert_element_type.302), calls=%async_computation.9 | async-start | bytes 1048576 | tf_op jit(solution)/shard_map/all_to_all | solution.py:283
  258.3 66.4 %all-reduce.6.cloned.1.call-start = ((), (), s32[]{:S(2)}) async-start(), calls=%async_computation.13 | async-start | bytes 2097152 | tf_op jit(solution)/shard_map/psum | solution.py:257
  269.5 62.6 %all-to-all-start.11 = ((bf16[16,32,512]{2,1,0:T(8,128)(2,1)}), bf16[16,32,512]{2,1,0:T(8,128)(2,1)S(1)}, u32[]{:S(2)}, u32[]{:S(2)}) async-start(bf16[16,32,512]{2,1,0:T(8,128)(2,1)} %all_to_all.151), calls=%async_computation.11 | async-start | bytes 1048576 | tf_op jit(solution)/shard_map/all_to_all | solution.py:274
  (23 other events, 104.6 us)
Sparse Core Ops, SparseCore 0:
  208.6 22.0 all-reduce.3
Sparse Core Ops, SparseCore 1:
  261.9 62.7 all-reduce.5

commit v2 on v1

--- a/solution.py
+++ b/solution.py
@@ -253,23 +253,33 @@
         + blockwise_back(value_back, value_weight)
     ).astype(jnp.bfloat16)
     factor = 1.0 / math.sqrt(lax.axis_size("dp") * length)
-    query_grad, key_grad, value_grad, output_grad = (
-        lax.psum(
-            (weight_term(inputs, query_back, blocks) * factor).astype(jnp.bfloat16),
-            ("dp", "context"),
-        ).astype(jnp.float32),
-        lax.psum(
-            (weight_term(inputs, key_back, blocks) * factor).astype(jnp.bfloat16), ("dp", "context")
-        ).astype(jnp.float32),
-        lax.psum(
-            (weight_term(inputs, value_back, blocks) * factor).astype(jnp.bfloat16),
-            ("dp", "context"),
-        ).astype(jnp.float32),
-        lax.psum(
-            (weight_term(weighted, upstream, blocks) * factor).astype(jnp.bfloat16),
-            ("dp", "context"),
-        ).astype(jnp.float32),
-    )
+    terms = jnp.stack(
+        [
+            weight_term(inputs, query_back, blocks),
+            weight_term(inputs, key_back, blocks),
+            weight_term(inputs, value_back, blocks),
+            weight_term(weighted, upstream, blocks),
+        ]
+    )
+    group = ("dp", "context")
+    members = lax.axis_size("dp") * lax.axis_size("context")
+    pieces = lax.all_to_all(
+        (terms * factor).astype(jnp.bfloat16).reshape(members, -1),
+        group,
+        split_axis=0,
+        concat_axis=0,
+        tiled=True,
+    )
+    own = jnp.sum(pieces.astype(jnp.float32), axis=0).astype(jnp.bfloat16)
+    gathered = lax.all_to_all(
+        jnp.broadcast_to(own[None], (members, own.shape[0])),
+        group,
+        split_axis=0,
+        concat_axis=0,
+        tiled=True,
+    )
+    summed = gathered.reshape(terms.shape).astype(jnp.float32)
+    query_grad, key_grad, value_grad, output_grad = summed[0], summed[1], summed[2], summed[3]
     taps_total = lax.psum((taps_back * factor).astype(jnp.bfloat16), "dp").astype(jnp.float32)
     filter_grad = lax.all_to_all(
         lax.all_to_all(

time: 347 us -> 358 us (1.032)
  waiting for transfers between devices: 116 us -> 83.8 us
  other arithmetic: 51.7 us -> 70.4 us
  local copies, waits for them, and re-layouts: 45.9 us -> 61.2 us
  starting transfers between devices: 52.3 us -> 64.8 us
  matrix products: 59 us -> 55.4 us
    psum x1 -> x0, waiting for transfers between devices: 47.9 us -> none  [shards(): lax.psum((weight_term(inputs, query_back, blocks) * factor).astype(jnp.bf...]
    all_to_all x0 -> x2, waiting for transfers between devices: none -> 21 us  [the longest x1 12.8 us: shards(): lax.all_to_all((terms * factor).astype(jnp.bfloat16).reshape(members, -1)...]
    all_to_all x0 -> x2, starting transfers between devices: none -> 8.85 us  [the longest x1 5.04 us: shards(): lax.all_to_all((terms * factor).astype(jnp.bfloat16).reshape(members, -1)...]
    convert_element_type x1 -> x3, other arithmetic: 1.78 us -> 10.4 us  [the longest x2 8.28 us: shards(): (terms * factor).astype(jnp.bfloat16).reshape(members, -1)]
    broadcast_in_dim x0 -> x1, other arithmetic: none -> 7.04 us  [shards(): jnp.broadcast_to(own[None], (members, own.shape[0]))]
    slice x0 -> x1, local copies, waits for them, and re-layouts: none -> 6.66 us  [shards(): summed[3]]
    all_to_all x1, waiting for transfers between devices: 5.01 us -> 0.01 us  [shards(): lax.all_to_all(taps_total.astype(jnp.bfloat16), 'context', split_axis=0,...]
    dot_general x4, matrix products: 6.11 us -> 2.04 us  [weight_term(): jnp.einsum('tni,tnj->nij', left, right, preferred_element_type=jnp.float32)]
  transfers between devices with their start and end apart: 14 -> 15, of which waited for: 11 -> 11; matrix products, arithmetic and copies ran while one was open for 15% -> 20% of each run, Pallas kernels for 0% -> 0%
where the time goes in v2:
time: 358 us; the launch traced here: 351 us
  waiting for transfers between devices  83.8 us (23%)
  other arithmetic  70.4 us (20%)
  starting transfers between devices  64.8 us (18%)
  local copies, waits for them, and re-layouts  61.2 us (17%)
  matrix products  55.4 us (15%)
  between operations  15.1 us (4%)
    dot_general x1, matrix products, spectra(): jnp.einsum('rkmc,rmsl->sklc', turned, forward_second, precision=table_mod...  20.4 us
    unnamed x62, local copies, waits for them, and re-layouts  13.9 us
    all_to_all x1, waiting for transfers between devices, shards(): lax.all_to_all((terms * factor).astype(jnp.bfloat16).reshape(members, -1)...  12.8 us
    dot_general x1, matrix products, signals(): jnp.einsum('nrk,rkmc->nmc', inverse_first, turned, precision=table_mode,...  12.3 us
    another operation x2, other arithmetic, spectra(): jnp.stack([real_section * cosine_twist + imag_section * sine_twist, imag_...  12.2 us
    all_to_all x1, waiting for transfers between devices, shards(): lax.all_to_all(filter_taps, 'tensor', split_axis=1, concat_axis=0, tiled=...  10.6 us
    all_to_all x1, waiting for transfers between devices, shards(): lax.all_to_all(out_cotangent[0], 'tensor', split_axis=1, concat_axis=0, t...  10.3 us
    all_to_all x1, waiting for transfers between devices, shards(): lax.all_to_all(tokens[0], 'tensor', split_axis=1, concat_axis=0, tiled=True)  9.24 us
  transfers between devices with their start and end apart: 15, of which 11 were waited for; matrix products, arithmetic and copies ran while one was open for 20% of the time, Pallas kernels for 0%

profile of v2, /device:TPU:0, one launch (start us, length us, event | category | flops | bytes accessed | tf_op | source)
XLA Modules:
  0.0 350.7 jit_solution(5465721949261819664)
XLA Ops:
  9.5 7.1 %all-to-all-start = ((bf16[32,16,512]{2,0,1:T(8,128)(2,1)}), bf16[32,16,512]{2,0,1:T(8,128)(2,1)S(1)}, u32[]{:S(2)}, u32[]{:S(2)}) async-start(bf16[32,16,512]{2,0,1:T(8,128)(2,1)} %copy.157), calls=%async_computation | async-start | bytes 1048576 | tf_op jit(solution)/shard_map/all_to_all | solution.py:176
  19.0 9.2 %all-to-all-done = bf16[32,16,512]{2,0,1:T(8,128)(2,1)S(1)} async-done(((bf16[32,16,512]{2,0,1:T(8,128)(2,1)}), bf16[32,16,512]{2,0,1:T(8,128)(2,1)S(1)}, u32[]{:S(2)}, u32[]{:S(2)}) %all-to-all-start) | async-done | bytes 524320 | tf_op jit(solution)/shard_map/all_to_all | solution.py:176
  32.0 10.3 %all-to-all-done.4 = bf16[32,16,512]{2,0,1:T(8,128)(2,1)S(1)} async-done(((bf16[32,16,512]{2,0,1:T(8,128)(2,1)}), bf16[32,16,512]{2,0,1:T(8,128)(2,1)S(1)}, u32[]{:S(2)}, u32[]{:S(2)}) %all-to-all-start.4) | async-done | bytes 524320 | tf_op jit(solution)/shard_map/all_to_all | solution.py:177
  46.0 5.3 %all-to-all-start.5 = ((bf16[512,4,128]{2,0,1:T(8,128)(2,1)}), bf16[512,4,128]{2,0,1:T(8,128)(2,1)S(1)}, u32[]{:S(2)}, u32[]{:S(2)}) async-start(bf16[512,4,128]{2,0,1:T(8,128)(2,1)} %copy.170), calls=%async_computation.5 | async-start | bytes 1048576 | tf_op jit(solution)/shard_map/all_to_all | solution.py:198
  53.7 5.8 %all-to-all-done.5 = bf16[512,4,128]{2,0,1:T(8,128)(2,1)S(1)} async-done(((bf16[512,4,128]{2,0,1:T(8,128)(2,1)}), bf16[512,4,128]{2,0,1:T(8,128)(2,1)S(1)}, u32[]{:S(2)}, u32[]{:S(2)}) %all-to-all-start.5) | async-done | bytes 524320 | tf_op jit(solution)/shard_map/all_to_all | solution.py:198
  66.8 10.6 %all-to-all-done.1 = f32[32,16,512]{2,0,1:T(8,128)S(1)} async-done(((f32[32,16,512]{2,0,1:T(8,128)}), f32[32,16,512]{2,0,1:T(8,128)S(1)}, u32[]{:S(2)}, u32[]{:S(2)}) %all-to-all-start.1) | async-done | bytes 1048608 | tf_op jit(solution)/shard_map/all_to_all | solution.py:186
  97.4 6.4 %all-to-all-done.2 = f32[512,4,128]{2,0,1:T(8,128)S(1)} async-done(((f32[512,4,128]{2,0,1:T(8,128)}), f32[512,4,128]{2,0,1:T(8,128)S(1)}, u32[]{:S(2)}, u32[]{:S(2)}) %all-to-all-start.2) | async-done | bytes 1048608 | tf_op jit(solution)/shard_map/all_to_all | solution.py:185
  104.4 5.2 %fusion.14 = f32[256,32,384]{2,0,1:T(8,128)S(1)} fusion(f32[64,32,128]{2,0,1:T(8,128)S(1)} %copy.173, f32[64,32,128]{2,0,1:T(8,128)S(1)} %copy.172, f32[64,32,128]{2,0,1:T(8,128)S(1)} %copy.171, f32[128,64]{1,0:T(8,128)S(1)} %copy-done.17, f32[128,64]{1,0:T(8,128)S(1)} %bitcast.215), kind=kOutput, calls=%fused_computation.21 | convolution fusion | flops 1209548800 | bytes 15794176 | tf_op jit(solution)/shard_map/kn,nmc->kmc/dot_general | solution.py:135
  113.3 8.5 %pad_maximum_fusion = f32[2,128,32,384]{3,1,2,0:T(8,128)} fusion(f32[1,128,32,384]{3,1,2,0:T(8,128)} %get-tuple-element.14, f32[1,128,32,384]{3,1,2,0:T(8,128)S(1)} %get-tuple-element.13), kind=kLoop, calls=%fused_computation | loop fusion | flops 3145728 | bytes 25165824 | tf_op jit(solution)/shard_map/stack | solution.py:140
  121.8 20.4 %fusion.8 = f32[2,128,32,384]{3,2,1,0:T(8,128)} fusion(f32[2,128,32,384]{3,1,2,0:T(8,128)} %pad_maximum_fusion, f32[1,32,2,32]{1,3,0,2:T(8,128)S(1)} %copy-done.24, f32[1,32,2,32]{1,3,0,2:T(8,128)S(1)} %copy-done.25), kind=kOutput, calls=%fused_computation.19 | convolution fusion | flops 1207963648 | bytes 25182208 | tf_op jit(solution)/shard_map/rkmc,rmsl->sklc/dot_general | solution.py:146
  142.2 8.6 %slice_bitcast_fusion.1 = (f32[128,32,384]{2,1,0:T(8,128)S(1)}, f32[128,32,384]{2,1,0:T(8,128)}) fusion(f32[2,128,32,384]{3,2,1,0:T(8,128)} %fusion.8), kind=kLoop, calls=%fused_computation.12 | loop fusion | bytes 25165824 | tf_op jit(solution)/shard_map/squeeze | solution.py:205
  150.8 8.0 %multiply_subtract_fusion.3 = (f32[128,32,128]{2,1,0:T(8,128)}, f32[128,32,128]{2,1,0:T(8,128)}, f32[128,32,128]{2,1,0:T(8,128)}, f32[128,32,128]{2,1,0:T(8,128)}) fusion(f32[128,32,384]{2,1,0:T(8,128)} %get-tuple-element.22, f32[128,32,384]{2,1,0:T(8,128)S(1)} %get-tuple-element.21), kind=kLoop, calls=%fused_computation.34 | loop fusion | flops 6291456 | bytes 20971520 | tf_op jit(solution)/shard_map/sub | solution.py:216
  165.4 5.6 %fusion.11 = f32[2,128,32,384]{3,2,1,0:T(8,128)S(1)} fusion(f32[1,128,32,384]{3,2,1,0:T(8,128)S(1)} %maximum_bitcast_fusion.1, f32[1,128,32,384]{3,2,1,0:T(8,128)S(1)} %maximum_bitcast_fusion, f32[1,32,2,32]{1,3,2,0:T(8,128)S(1)} %copy-done.23, f32[1,32,2,32]{1,3,2,0:T(8,128)S(1)} %copy-done.22), kind=kOutput, calls=%fused_computation.20 | convolution fusion | flops 1211109376 | bytes 25182208 | tf_op jit(solution)/shard_map/sklc,slrm->rkmc/dot_general | solution.py:154
  175.1 8.7 %pad_maximum_fusion.2 = f32[2,128,32,384]{3,2,1,0:T(8,128)} fusion(f32[1,128,32,384]{3,2,1,0:T(8,128)} %get-tuple-element.12, f32[1,128,32,384]{3,2,1,0:T(8,128)S(1)} %get-tuple-element.11), kind=kLoop, calls=%fused_computation.2 | loop fusion | flops 3145728 | bytes 25165824 | tf_op jit(solution)/shard_map/stack | solution.py:159
  183.8 12.3 %fusion.21 = f32[64,32,384]{2,0,1:T(8,128)S(1)} fusion(f32[2,128,32,384]{3,2,1,0:T(8,128)} %pad_maximum_fusion.2, f32[64,1,128]{2,0,1:T(8,128)S(1)} %copy-done.20, f32[64,1,128]{2,0,1:T(8,128)S(1)} %copy-done.21), kind=kOutput, calls=%fused_computation.35 | convolution fusion | flops 1207992320 | bytes 15794176 | tf_op jit(solution)/shard_map/nrk,rkmc->nmc/dot_general | solution.py:165
  204.2 7.2 %all-to-all-done.6 = bf16[4,512,128]{2,1,0:T(8,128)(2,1)} async-done(((bf16[4,512,128]{2,1,0:T(8,128)(2,1)}), bf16[4,512,128]{2,1,0:T(8,128)(2,1)}, u32[]{:S(2)}, u32[]{:S(2)}) %all-to-all-start.6) | async-done | bytes 524320 | tf_op jit(solution)/shard_map/all_to_all | solution.py:236
  238.8 7.3 %all-to-all-start.9 = ((bf16[16,32,512]{2,1,0:T(8,128)(2,1)}), bf16[16,32,512]{2,1,0:T(8,128)(2,1)}, u32[]{:S(2)}, u32[]{:S(2)}) async-start(bf16[16,32,512]{2,1,0:T(8,128)(2,1)} %convert_element_type.289), calls=%async_computation.9 | async-start | bytes 1048576 | tf_op jit(solution)/shard_map/all_to_all | solution.py:293
  247.6 8.7 %all-to-all-done.9 = bf16[16,32,512]{2,1,0:T(8,128)(2,1)} async-done(((bf16[16,32,512]{2,1,0:T(8,128)(2,1)}), bf16[16,32,512]{2,1,0:T(8,128)(2,1)}, u32[]{:S(2)}, u32[]{:S(2)}) %all-to-all-start.9) | async-done | bytes 524320 | tf_op jit(solution)/shard_map/all_to_all | solution.py:293
  264.2 7.0 %reduce.10 = bf16[8,65536]{1,0:T(8,128)(2,1)S(1)} reduce(bf16[8,1,65536]{2,1,0:T(2,128)(2,1)S(1)} %convert_element_type.310, bf16[]{:T(256)} %broadcast.209), dimensions={1}, to_apply=%convert_element_type.310.reduce_sub_computation | reduce | bytes 2097154 | tf_op jit(solution)/shard_map/convert_element_type | solution.py:267
  273.1 5.0 %all-to-all-start.12 = ((bf16[8,2,32768]{2,1,0:T(2,128)(2,1)}), bf16[8,2,32768]{2,1,0:T(2,128)(2,1)S(1)}, u32[]{:S(2)}, u32[]{:S(2)}) async-start(bf16[8,2,32768]{2,1,0:T(2,128)(2,1)} %reshape.301), calls=%async_computation.12 | async-start | bytes 2097152 | tf_op jit(solution)/shard_map/all_to_all | solution.py:266
  280.6 12.8 %all-to-all-done.12 = bf16[8,2,32768]{2,1,0:T(2,128)(2,1)S(1)} async-done(((bf16[8,2,32768]{2,1,0:T(2,128)(2,1)}), bf16[8,2,32768]{2,1,0:T(2,128)(2,1)S(1)}, u32[]{:S(2)}, u32[]{:S(2)}) %all-to-all-start.12) | async-done | bytes 1048608 | tf_op jit(solution)/shard_map/all_to_all | solution.py:266
  302.2 7.0 %reduce.11 = bf16[8,65536]{1,0:T(8,128)(2,1)S(1)} reduce(bf16[8,1,65536]{2,1,0:T(2,128)(2,1)S(1)} %broadcast_in_dim.8, bf16[]{:T(256)} %broadcast.209), dimensions={1}, to_apply=%broadcast_in_dim.8.reduce_sub_computation | reduce | bytes 2097154 | tf_op jit(solution)/shard_map/broadcast_in_dim | solution.py:275
  322.0 8.2 %all-to-all-done.13 = bf16[8,2,32768]{2,1,0:T(2,128)(2,1)S(1)} async-done(((bf16[8,2,32768]{2,1,0:T(2,128)(2,1)}), bf16[8,2,32768]{2,1,0:T(2,128)(2,1)S(1)}, u32[]{:S(2)}, u32[]{:S(2)}) %all-to-all-start.13) | async-done | bytes 1048608 | tf_op jit(solution)/shard_map/all_to_all | solution.py:274
  333.4 6.7 %slice_reduce_fusion = (f32[2,65536]{1,0:T(2,128)S(1)}, f32[2,65536]{1,0:T(2,128)S(1)}, f32[2,65536]{1,0:T(2,128)S(1)}, f32[2,65536]{1,0:T(2,128)S(1)}) fusion(f32[8,1,65536]{2,1,0:T(1,128)S(1)} %convert_element_type.296), kind=kLoop, calls=%fused_computation.75 | loop fusion | bytes 4194304 | tf_op jit(solution)/shard_map/slice | solution.py:282
  (150 shorter events, 133.6 us)
Async XLA Ops:
  7.2 36.6 %copy-start = (bf16[2,256,256]{2,1,0:T(8,128)(2,1)S(1)}, bf16[2,256,256]{2,1,0:T(8,128)(2,1)}, u32[]{:S(2)}) copy-start(bf16[2,256,256]{2,1,0:T(8,128)(2,1)} %param.12) | copy-start | bytes 786436
  7.2 35.2 %copy-start.13 = (bf16[2,256,256]{2,1,0:T(8,128)(2,1)S(1)}, bf16[2,256,256]{2,1,0:T(8,128)(2,1)}, u32[]{:S(2)}) copy-start(bf16[2,256,256]{2,1,0:T(8,128)(2,1)} %param.9) | copy-start | bytes 786436
  9.5 18.7 %all-to-all-start = ((bf16[32,16,512]{2,0,1:T(8,128)(2,1)}), bf16[32,16,512]{2,0,1:T(8,128)(2,1)S(1)}, u32[]{:S(2)}, u32[]{:S(2)}) async-start(bf16[32,16,512]{2,0,1:T(8,128)(2,1)} %copy.157), calls=%async_computation | async-start | bytes 1048576 | tf_op jit(solution)/shard_map/all_to_all | solution.py:176
  28.2 14.0 %all-to-all-start.4 = ((bf16[32,16,512]{2,0,1:T(8,128)(2,1)}), bf16[32,16,512]{2,0,1:T(8,128)(2,1)S(1)}, u32[]{:S(2)}, u32[]{:S(2)}) async-start(bf16[32,16,512]{2,0,1:T(8,128)(2,1)} %copy.168), calls=%async_computation.4 | async-start | bytes 1048576 | tf_op jit(solution)/shard_map/all_to_all | solution.py:177
  31.9 31.5 %copy-start.2 = (bf16[512,2,256]{2,1,0:T(2,128)(2,1)}, bf16[512,2,256]{2,1,0:T(2,128)(2,1)S(1)}, u32[]{:S(2)}) copy-start(bf16[512,2,256]{2,1,0:T(2,128)(2,1)S(1)} %reshape.280) | copy-start | bytes 1572868
  42.2 20.9 %copy-start.14 = (bf16[2,256,256]{2,1,0:T(8,128)(2,1)S(1)}, bf16[2,256,256]{2,1,0:T(8,128)(2,1)}, u32[]{:S(2)}) copy-start(bf16[2,256,256]{2,1,0:T(8,128)(2,1)} %param.10) | copy-start | bytes 786436
  42.4 21.1 %copy-start.9 = (bf16[512,2,256]{2,1,0:T(2,128)(2,1)}, bf16[512,2,256]{2,1,0:T(2,128)(2,1)S(1)}, u32[]{:S(2)}) copy-start(bf16[512,2,256]{2,1,0:T(2,128)(2,1)S(1)} %reshape.281) | copy-start | bytes 1572868
  46.0 13.4 %all-to-all-start.5 = ((bf16[512,4,128]{2,0,1:T(8,128)(2,1)}), bf16[512,4,128]{2,0,1:T(8,128)(2,1)S(1)}, u32[]{:S(2)}, u32[]{:S(2)}) async-start(bf16[512,4,128]{2,0,1:T(8,128)(2,1)} %copy.170), calls=%async_computation.5 | async-start | bytes 1048576 | tf_op jit(solution)/shard_map/all_to_all | solution.py:198
  59.4 17.9 %all-to-all-start.1 = ((f32[32,16,512]{2,0,1:T(8,128)}), f32[32,16,512]{2,0,1:T(8,128)S(1)}, u32[]{:S(2)}, u32[]{:S(2)}) async-start(f32[32,16,512]{2,0,1:T(8,128)} %bitcast.179), calls=%async_computation.1 | async-start | bytes 2097152 | tf_op jit(solution)/shard_map/all_to_all | solution.py:186
  77.4 11.5 %all-to-all-start.3 = ((bf16[512,4,128]{2,0,1:T(8,128)(2,1)}), bf16[512,4,128]{2,0,1:T(8,128)(2,1)S(1)}, u32[]{:S(2)}, u32[]{:S(2)}) async-start(bf16[512,4,128]{2,0,1:T(8,128)(2,1)} %copy.167), calls=%async_computation.3 | async-start | bytes 1048576 | tf_op jit(solution)/shard_map/all_to_all | solution.py:195
  80.9 12.0 %copy-start.18 = (f32[128,32]{0,1:T(8,128)}, f32[128,32]{0,1:T(8,128)S(1)}, u32[]{:S(2)}) copy-start(f32[128,32]{0,1:T(8,128)S(1)} %get-tuple-element.40) | copy-start | bytes 49156
  88.9 14.9 %all-to-all-start.2 = ((f32[512,4,128]{2,0,1:T(8,128)}), f32[512,4,128]{2,0,1:T(8,128)S(1)}, u32[]{:S(2)}, u32[]{:S(2)}) async-start(f32[512,4,128]{2,0,1:T(8,128)} %copy.162), calls=%async_computation.2 | async-start | bytes 2097152 | tf_op jit(solution)/shard_map/all_to_all | solution.py:185
  199.1 12.3 %all-to-all-start.6 = ((bf16[4,512,128]{2,1,0:T(8,128)(2,1)}), bf16[4,512,128]{2,1,0:T(8,128)(2,1)}, u32[]{:S(2)}, u32[]{:S(2)}) async-start(bf16[4,512,128]{2,1,0:T(8,128)(2,1)} %bitcast.200), calls=%async_computation.6 | async-start | bytes 1048576 | tf_op jit(solution)/shard_map/all_to_all | solution.py:236
  203.3 44.3 %all-reduce.2.cloned.1.call-start = ((), (), s32[]{:S(2)}) async-start(), calls=%async_computation.14 | async-start | bytes 1048576 | tf_op jit(solution)/shard_map/psum | solution.py:283
  211.4 12.3 %all-to-all-start.8 = ((bf16[4,512,128]{2,1,0:T(8,128)(2,1)}), bf16[4,512,128]{2,1,0:T(8,128)(2,1)}, u32[]{:S(2)}, u32[]{:S(2)}) async-start(bf16[4,512,128]{2,1,0:T(8,128)(2,1)} %bitcast.199), calls=%async_computation.8 | async-start | bytes 1048576 | tf_op jit(solution)/shard_map/all_to_all | solution.py:239
  217.0 13.6 %copy-start.12 = (bf16[2,256,512]{2,1,0:T(8,128)(2,1)S(1)}, bf16[2,256,512]{2,1,0:T(8,128)(2,1)}, u32[]{:S(2)}) copy-start(bf16[2,256,512]{2,1,0:T(8,128)(2,1)} %copy-done.11) | copy-start | bytes 1572868
  223.7 15.1 %all-to-all-start.7 = ((bf16[16,32,512]{2,1,0:T(8,128)(2,1)}), bf16[16,32,512]{2,1,0:T(8,128)(2,1)}, u32[]{:S(2)}, u32[]{:S(2)}) async-start(bf16[16,32,512]{2,1,0:T(8,128)(2,1)} %convert_element_type.276), calls=%async_computation.7 | async-start | bytes 1048576 | tf_op jit(solution)/shard_map/all_to_all | solution.py:245
  230.6 15.5 %copy-start.3 = (bf16[512,2,256]{2,1,0:T(2,128)(2,1)S(1)}, bf16[512,2,256]{2,1,0:T(2,128)(2,1)}, u32[]{:S(2)}) copy-start(bf16[512,2,256]{2,1,0:T(2,128)(2,1)} %copy-done.2) | copy-start | bytes 1572868
  232.3 28.4 %copy-start.10 = (bf16[512,2,256]{2,1,0:T(2,128)(2,1)S(1)}, bf16[512,2,256]{2,1,0:T(2,128)(2,1)}, u32[]{:S(2)}) copy-start(bf16[512,2,256]{2,1,0:T(2,128)(2,1)} %copy-done.9) | copy-start | bytes 1572868
  238.8 17.5 %all-to-all-start.9 = ((bf16[16,32,512]{2,1,0:T(8,128)(2,1)}), bf16[16,32,512]{2,1,0:T(8,128)(2,1)}, u32[]{:S(2)}, u32[]{:S(2)}) async-start(bf16[16,32,512]{2,1,0:T(8,128)(2,1)} %convert_element_type.289), calls=%async_computation.9 | async-start | bytes 1048576 | tf_op jit(solution)/shard_map/all_to_all | solution.py:293
  256.3 16.8 %all-to-all-start.10 = ((bf16[4,512,128]{2,1,0:T(8,128)(2,1)}), bf16[4,512,128]{2,1,0:T(8,128)(2,1)}, u32[]{:S(2)}, u32[]{:S(2)}) async-start(bf16[4,512,128]{2,1,0:T(8,128)(2,1)} %all-reduce.2.cloned.1.call-done), calls=%async_computation.10 | async-start | bytes 1048576 | tf_op jit(solution)/shard_map/all_to_all | solution.py:285
  273.1 20.3 %all-to-all-start.12 = ((bf16[8,2,32768]{2,1,0:T(2,128)(2,1)}), bf16[8,2,32768]{2,1,0:T(2,128)(2,1)S(1)}, u32[]{:S(2)}, u32[]{:S(2)}) async-start(bf16[8,2,32768]{2,1,0:T(2,128)(2,1)} %reshape.301), calls=%async_computation.12 | async-start | bytes 2097152 | tf_op jit(solution)/shard_map/all_to_all | solution.py:266
  293.4 17.8 %all-to-all-start.11 = ((bf16[16,32,512]{2,1,0:T(8,128)(2,1)}), bf16[16,32,512]{2,1,0:T(8,128)(2,1)}, u32[]{:S(2)}, u32[]{:S(2)}) async-start(bf16[16,32,512]{2,1,0:T(8,128)(2,1)} %all_to_all.159), calls=%async_computation.11 | async-start | bytes 1048576 | tf_op jit(solution)/shard_map/all_to_all | solution.py:284
  311.2 19.0 %all-to-all-start.13 = ((bf16[8,2,32768]{2,1,0:T(2,128)(2,1)}), bf16[8,2,32768]{2,1,0:T(2,128)(2,1)S(1)}, u32[]{:S(2)}, u32[]{:S(2)}) async-start(bf16[8,2,32768]{2,1,0:T(2,128)(2,1)} %reshape.303), calls=%async_computation.13 | async-start | bytes 2097152 | tf_op jit(solution)/shard_map/all_to_all | solution.py:274
  (17 other events, 82.4 us)
Sparse Core Ops, SparseCore 0:
  207.1 22.0 all-reduce.1
